TPU v7x, 32 devices: a whole 2x2x4 slice. The times are simulated.
32 devices in a mesh: groups: 2 (over x), chan: 16 (over z, y, core).
Axes of the slice: x: 2, y: 2, z: 4, core: 2. Of those that a mesh axis runs over, the one named last changes fastest.
Arguments:
- traces: float32 [2048, 1152], P(('groups', 'chan')), parts along dimension 0, as said below
- good_mask: int32 [2048], P(('groups', 'chan')), parts along dimension 0, may hold values 0 or 1
Outputs:
- correlations: bfloat16 [2048, 64, 1024], P(('groups', 'chan')), parts along dimension 0
There are 2 independent parts, one for each index of `groups`. A program takes and returns all parts, laid end to end along the dimension named above; each array names one. Nothing has to cross between parts.
Inputs may be any that keep to these rules, and one draw needn't show every extreme that they name: `traces`: traces of order one.
All inputs are finite; a program needn't handle non-finite values. No bound on the sum of `good_mask` on one device may be relied on, other than what follows from the above.
Results may differ from a plain program's by a relative error of at most 0.0053.
Values may be sent and summed in bfloat16 or wider, within the bound.
No kernel may reach another device: no remote copies, remote signals or barrier semaphores. Data moves between devices by JAX's collectives and lax.ppermute only.
A program may use at most 128 MiB of HBM per device.

v0:
```python
import math
import jax
import jax.numpy as jnp
from jax import lax
from jax.sharding import PartitionSpec as P

NW = 256
NF = 128
HOP = 128
LAGS = 64
NWIN = 8


def spread(value, axis, root):
    mine = lax.axis_index(axis) == root
    return lax.psum(jnp.where(mine, value, jnp.zeros_like(value)), axis)


def forward_table(width, bins):
    samples = jnp.arange(width)
    freqs = jnp.arange(1, bins + 1)
    phase = samples[:, None] * freqs[None, :] % width
    theta = 2.0 * math.pi * phase.astype(jnp.float32) / width
    hann = 0.5 - 0.5 * jnp.cos(2.0 * math.pi * samples.astype(jnp.float32) / width)
    return jnp.concatenate(
        [hann[:, None] * jnp.cos(theta), -hann[:, None] * jnp.sin(theta)], axis=1
    )


def lag_table(width, bins, lag_count):
    freqs = jnp.arange(1, bins + 1)
    lags = jnp.arange(lag_count) - lag_count // 2
    phase = freqs[:, None] * lags[None, :] % width
    theta = 2.0 * math.pi * phase.astype(jnp.float32) / width
    return (jnp.concatenate([jnp.cos(theta), -jnp.sin(theta)], axis=0) / bins).astype(jnp.bfloat16)


def pair_block(own, other, table, windows):
    bins = own.shape[2] // 2
    own_real, own_imag = (own[..., :bins], own[..., bins:])
    other_real, other_imag = (other[..., :bins], other[..., bins:])

    def product(left, right):
        return jnp.einsum("wif,wjf->ijf", left, right, preferred_element_type=jnp.float32)

    real_sum = product(own_real, other_real) + product(own_imag, other_imag)
    imag_sum = product(own_imag, other_real) - product(own_real, other_imag)
    stack = (jnp.concatenate([real_sum, imag_sum], axis=2) / windows).astype(jnp.bfloat16)
    result = jnp.einsum("ijk,kl->ilj", stack, table, preferred_element_type=jnp.float32)
    return result.astype(jnp.bfloat16)


def shards(traces, good_mask):
    channels_here = traces.shape[0]
    windows = NWIN
    good = good_mask.astype(jnp.float32)
    total, count = lax.psum((jnp.sum(traces * good[:, None], axis=0), jnp.sum(good)), "chan")
    common = total / jnp.maximum(count, 1.0)
    clean = (traces - common[None, :]) * good[:, None]
    halves = clean.reshape(channels_here, windows + 1, HOP)
    segments = jnp.concatenate([halves[:, :-1], halves[:, 1:]], axis=2)
    spectrum = jnp.einsum(
        "cwn,nk->wck", segments, forward_table(NW, NF), precision=lax.Precision.HIGHEST
    )
    real_part = spectrum[..., :NF]
    imag_part = spectrum[..., NF:]
    power = real_part * real_part + imag_part * imag_part
    magnitude = jnp.sqrt(power)
    level = jnp.sqrt(jnp.mean(power, axis=-1, keepdims=True) + 1e-06)
    denom = jnp.maximum(magnitude, 0.3 * level)
    whitened = jnp.concatenate([real_part / denom, imag_part / denom], axis=-1).astype(jnp.bfloat16)
    table = lag_table(NW, NF, LAGS)
    owners = lax.axis_size("chan")
    result = jnp.zeros((channels_here, LAGS, channels_here * owners), jnp.bfloat16)

    def visit(owner, current):
        other = spread(whitened, "chan", owner)
        block = pair_block(whitened, other, table, windows)
        start = (owner * channels_here).astype(jnp.int32)
        return lax.dynamic_update_slice(current, block, (jnp.int32(0), jnp.int32(0), start))

    result = lax.fori_loop(0, owners, visit, result)
    return result


def solution(mesh):
    placed = (P(("groups", "chan"), None), P(("groups", "chan")))
    return jax.shard_map(
        shards,
        mesh=mesh,
        in_specs=placed,
        out_specs=P(("groups", "chan"), None, None),
        check_vma=False,
    )
```

profile of v0, /device:TPU:0, one launch (start us, length us, event | category | flops | bytes accessed | tf_op | source)
XLA Modules:
  0.0 2380.2 jit_solution(5177793545426857006)
XLA Ops:
  9.5 36.6 %all-reduce = (f32[1152]{0:T(1024)S(1)}, f32[]{:T(128)}) all-reduce(f32[1152]{0:T(1024)S(1)} %multiply_reduce_fusion, f32[]{:T(128)} %convert_reduce_fusion), channel_id=1, replica_groups=mesh['groups'=2,'chan'=16] {'chan'}, use_global_device_ids=true, to_apply=%region_1.0 | all-reduce | flops 1153 | bytes 9224 | tf_op jit(solution)/shard_map/psum | solution.py:57
  54.4 2319.3 %while.13 = (s32[]{:T(128)}, bf16[64,64,1024]{2,1,0:T(8,128)(2,1)}, bf16[8,64,256]{2,1,0:T(8,128)(2,1)S(1)}, bf16[256,64]{0,1:T(8,128)(2,1)S(1)}, s32[]{:T(128)}...) while((s32[]{:T(128)}, bf16[64,64,1024]{2,1,0:T(8,128)(2,1)}, bf16[8,64,256]{2,1,0:T(8,128)(2,1)S(1)}, ...), condition=%wide.region_7.8_spmd, body=%wide.region_5.7_spmd.sunk | while | flops 172490752 | bytes 48791760 | solution.py:82
  55.6 90.0 %all-reduce.3.cloned.1.call-done = bf16[8,64,256]{2,1,0:T(8,128)(2,1)} async-done(((bf16[8,64,256]{2,1,0:T(8,128)(2,1)}), bf16[8,64,256]{2,1,0:T(8,128)(2,1)}) %all-reduce.3.cloned.1.call-update) | async-done | bytes 262160 | tf_op jit(solution)/shard_map/while/body/eval_jaxpr/psum | solution.py:16
  162.4 5.4 copy.28
  183.2 10.6 dynamic_update_slice.8
  195.0 93.3 %all-reduce.3.cloned.1.call-done = bf16[8,64,256]{2,1,0:T(8,128)(2,1)} async-done(((bf16[8,64,256]{2,1,0:T(8,128)(2,1)}), bf16[8,64,256]{2,1,0:T(8,128)(2,1)}) %all-reduce.3.cloned.1.call-update) | async-done | bytes 262160 | tf_op jit(solution)/shard_map/while/body/eval_jaxpr/psum | solution.py:16
  305.0 5.4 copy.28
  325.9 16.0 dynamic_update_slice.8
  343.2 93.3 %all-reduce.3.cloned.1.call-done = bf16[8,64,256]{2,1,0:T(8,128)(2,1)} async-done(((bf16[8,64,256]{2,1,0:T(8,128)(2,1)}), bf16[8,64,256]{2,1,0:T(8,128)(2,1)}) %all-reduce.3.cloned.1.call-update) | async-done | bytes 262160 | tf_op jit(solution)/shard_map/while/body/eval_jaxpr/psum | solution.py:16
  453.2 5.4 copy.28
  474.1 10.6 dynamic_update_slice.8
  485.8 92.9 %all-reduce.3.cloned.1.call-done = bf16[8,64,256]{2,1,0:T(8,128)(2,1)} async-done(((bf16[8,64,256]{2,1,0:T(8,128)(2,1)}), bf16[8,64,256]{2,1,0:T(8,128)(2,1)}) %all-reduce.3.cloned.1.call-update) | async-done | bytes 262160 | tf_op jit(solution)/shard_map/while/body/eval_jaxpr/psum | solution.py:16
  595.5 5.4 copy.28
  616.4 16.0 dynamic_update_slice.8
  633.7 92.9 %all-reduce.3.cloned.1.call-done = bf16[8,64,256]{2,1,0:T(8,128)(2,1)} async-done(((bf16[8,64,256]{2,1,0:T(8,128)(2,1)}), bf16[8,64,256]{2,1,0:T(8,128)(2,1)}) %all-reduce.3.cloned.1.call-update) | async-done | bytes 262160 | tf_op jit(solution)/shard_map/while/body/eval_jaxpr/psum | solution.py:16
  743.4 5.4 copy.28
  764.2 10.6 dynamic_update_slice.8
  776.0 92.9 %all-reduce.3.cloned.1.call-done = bf16[8,64,256]{2,1,0:T(8,128)(2,1)} async-done(((bf16[8,64,256]{2,1,0:T(8,128)(2,1)}), bf16[8,64,256]{2,1,0:T(8,128)(2,1)}) %all-reduce.3.cloned.1.call-update) | async-done | bytes 262160 | tf_op jit(solution)/shard_map/while/body/eval_jaxpr/psum | solution.py:16
  885.7 5.4 copy.28
  906.6 16.0 dynamic_update_slice.8
  923.9 93.3 %all-reduce.3.cloned.1.call-done = bf16[8,64,256]{2,1,0:T(8,128)(2,1)} async-done(((bf16[8,64,256]{2,1,0:T(8,128)(2,1)}), bf16[8,64,256]{2,1,0:T(8,128)(2,1)}) %all-reduce.3.cloned.1.call-update) | async-done | bytes 262160 | tf_op jit(solution)/shard_map/while/body/eval_jaxpr/psum | solution.py:16
  1033.9 5.4 copy.28
  1054.8 10.6 dynamic_update_slice.8
  1066.5 93.3 %all-reduce.3.cloned.1.call-done = bf16[8,64,256]{2,1,0:T(8,128)(2,1)} async-done(((bf16[8,64,256]{2,1,0:T(8,128)(2,1)}), bf16[8,64,256]{2,1,0:T(8,128)(2,1)}) %all-reduce.3.cloned.1.call-update) | async-done | bytes 262160 | tf_op jit(solution)/shard_map/while/body/eval_jaxpr/psum | solution.py:16
  1176.5 5.4 copy.28
  1197.4 16.0 dynamic_update_slice.8
  1214.7 93.3 %all-reduce.3.cloned.1.call-done = bf16[8,64,256]{2,1,0:T(8,128)(2,1)} async-done(((bf16[8,64,256]{2,1,0:T(8,128)(2,1)}), bf16[8,64,256]{2,1,0:T(8,128)(2,1)}) %all-reduce.3.cloned.1.call-update) | async-done | bytes 262160 | tf_op jit(solution)/shard_map/while/body/eval_jaxpr/psum | solution.py:16
  1324.7 5.4 copy.28
  1345.6 10.6 dynamic_update_slice.8
  1357.3 92.9 %all-reduce.3.cloned.1.call-done = bf16[8,64,256]{2,1,0:T(8,128)(2,1)} async-done(((bf16[8,64,256]{2,1,0:T(8,128)(2,1)}), bf16[8,64,256]{2,1,0:T(8,128)(2,1)}) %all-reduce.3.cloned.1.call-update) | async-done | bytes 262160 | tf_op jit(solution)/shard_map/while/body/eval_jaxpr/psum | solution.py:16
  1467.0 5.4 copy.28
  1487.9 16.0 dynamic_update_slice.8
  1505.2 93.3 %all-reduce.3.cloned.1.call-done = bf16[8,64,256]{2,1,0:T(8,128)(2,1)} async-done(((bf16[8,64,256]{2,1,0:T(8,128)(2,1)}), bf16[8,64,256]{2,1,0:T(8,128)(2,1)}) %all-reduce.3.cloned.1.call-update) | async-done | bytes 262160 | tf_op jit(solution)/shard_map/while/body/eval_jaxpr/psum | solution.py:16
  1615.2 5.4 copy.28
  1636.1 10.6 dynamic_update_slice.8
  1647.8 92.9 %all-reduce.3.cloned.1.call-done = bf16[8,64,256]{2,1,0:T(8,128)(2,1)} async-done(((bf16[8,64,256]{2,1,0:T(8,128)(2,1)}), bf16[8,64,256]{2,1,0:T(8,128)(2,1)}) %all-reduce.3.cloned.1.call-update) | async-done | bytes 262160 | tf_op jit(solution)/shard_map/while/body/eval_jaxpr/psum | solution.py:16
  1757.5 5.4 copy.28
  1778.4 16.0 dynamic_update_slice.8
  1795.7 93.3 %all-reduce.3.cloned.1.call-done = bf16[8,64,256]{2,1,0:T(8,128)(2,1)} async-done(((bf16[8,64,256]{2,1,0:T(8,128)(2,1)}), bf16[8,64,256]{2,1,0:T(8,128)(2,1)}) %all-reduce.3.cloned.1.call-update) | async-done | bytes 262160 | tf_op jit(solution)/shard_map/while/body/eval_jaxpr/psum | solution.py:16
  1905.7 5.4 copy.28
  1926.6 10.6 dynamic_update_slice.8
  1938.3 92.9 %all-reduce.3.cloned.1.call-done = bf16[8,64,256]{2,1,0:T(8,128)(2,1)} async-done(((bf16[8,64,256]{2,1,0:T(8,128)(2,1)}), bf16[8,64,256]{2,1,0:T(8,128)(2,1)}) %all-reduce.3.cloned.1.call-update) | async-done | bytes 262160 | tf_op jit(solution)/shard_map/while/body/eval_jaxpr/psum | solution.py:16
  2068.9 16.0 dynamic_update_slice.8
  2086.2 93.0 %all-reduce.3.cloned.1.call-done = bf16[8,64,256]{2,1,0:T(8,128)(2,1)} async-done(((bf16[8,64,256]{2,1,0:T(8,128)(2,1)}), bf16[8,64,256]{2,1,0:T(8,128)(2,1)}) %all-reduce.3.cloned.1.call-update) | async-done | bytes 262160 | tf_op jit(solution)/shard_map/while/body/eval_jaxpr/psum | solution.py:16
  2216.8 9.9 dynamic_update_slice.8
  2227.8 92.9 %all-reduce.3.cloned.1.call-done = bf16[8,64,256]{2,1,0:T(8,128)(2,1)} async-done(((bf16[8,64,256]{2,1,0:T(8,128)(2,1)}), bf16[8,64,256]{2,1,0:T(8,128)(2,1)}) %all-reduce.3.cloned.1.call-update) | async-done | bytes 262160 | tf_op jit(solution)/shard_map/while/body/eval_jaxpr/psum | solution.py:16
  2337.5 5.4 copy.28
  2358.4 15.3 dynamic_update_slice.8
  (311 shorter events, 555.9 us)
Async XLA Ops:
  54.4 91.2 %all-reduce.3.cloned.1.call-start = ((), (), s32[]{:S(2)}) async-start(), calls=%async_computation | async-start | bytes 524288 | tf_op jit(solution)/shard_map/while/body/eval_jaxpr/psum | solution.py:16
  193.8 94.5 %all-reduce.3.cloned.1.call-start = ((), (), s32[]{:S(2)}) async-start(), calls=%async_computation | async-start | bytes 524288 | tf_op jit(solution)/shard_map/while/body/eval_jaxpr/psum | solution.py:16
  342.0 94.5 %all-reduce.3.cloned.1.call-start = ((), (), s32[]{:S(2)}) async-start(), calls=%async_computation | async-start | bytes 524288 | tf_op jit(solution)/shard_map/while/body/eval_jaxpr/psum | solution.py:16
  484.6 94.2 %all-reduce.3.cloned.1.call-start = ((), (), s32[]{:S(2)}) async-start(), calls=%async_computation | async-start | bytes 524288 | tf_op jit(solution)/shard_map/while/body/eval_jaxpr/psum | solution.py:16
  632.5 94.2 %all-reduce.3.cloned.1.call-start = ((), (), s32[]{:S(2)}) async-start(), calls=%async_computation | async-start | bytes 524288 | tf_op jit(solution)/shard_map/while/body/eval_jaxpr/psum | solution.py:16
  774.8 94.2 %all-reduce.3.cloned.1.call-start = ((), (), s32[]{:S(2)}) async-start(), calls=%async_computation | async-start | bytes 524288 | tf_op jit(solution)/shard_map/while/body/eval_jaxpr/psum | solution.py:16
  922.6 94.5 %all-reduce.3.cloned.1.call-start = ((), (), s32[]{:S(2)}) async-start(), calls=%async_computation | async-start | bytes 524288 | tf_op jit(solution)/shard_map/while/body/eval_jaxpr/psum | solution.py:16
  1065.3 94.5 %all-reduce.3.cloned.1.call-start = ((), (), s32[]{:S(2)}) async-start(), calls=%async_computation | async-start | bytes 524288 | tf_op jit(solution)/shard_map/while/body/eval_jaxpr/psum | solution.py:16
  1213.5 94.5 %all-reduce.3.cloned.1.call-start = ((), (), s32[]{:S(2)}) async-start(), calls=%async_computation | async-start | bytes 524288 | tf_op jit(solution)/shard_map/while/body/eval_jaxpr/psum | solution.py:16
  1356.1 94.2 %all-reduce.3.cloned.1.call-start = ((), (), s32[]{:S(2)}) async-start(), calls=%async_computation | async-start | bytes 524288 | tf_op jit(solution)/shard_map/while/body/eval_jaxpr/psum | solution.py:16
  1504.0 94.5 %all-reduce.3.cloned.1.call-start = ((), (), s32[]{:S(2)}) async-start(), calls=%async_computation | async-start | bytes 524288 | tf_op jit(solution)/shard_map/while/body/eval_jaxpr/psum | solution.py:16
  1646.6 94.2 %all-reduce.3.cloned.1.call-start = ((), (), s32[]{:S(2)}) async-start(), calls=%async_computation | async-start | bytes 524288 | tf_op jit(solution)/shard_map/while/body/eval_jaxpr/psum | solution.py:16
  1794.5 94.5 %all-reduce.3.cloned.1.call-start = ((), (), s32[]{:S(2)}) async-start(), calls=%async_computation | async-start | bytes 524288 | tf_op jit(solution)/shard_map/while/body/eval_jaxpr/psum | solution.py:16
  1937.1 94.2 %all-reduce.3.cloned.1.call-start = ((), (), s32[]{:S(2)}) async-start(), calls=%async_computation | async-start | bytes 524288 | tf_op jit(solution)/shard_map/while/body/eval_jaxpr/psum | solution.py:16
  2085.0 94.2 %all-reduce.3.cloned.1.call-start = ((), (), s32[]{:S(2)}) async-start(), calls=%async_computation | async-start | bytes 524288 | tf_op jit(solution)/shard_map/while/body/eval_jaxpr/psum | solution.py:16
  2226.6 94.2 %all-reduce.3.cloned.1.call-start = ((), (), s32[]{:S(2)}) async-start(), calls=%async_computation | async-start | bytes 524288 | tf_op jit(solution)/shard_map/while/body/eval_jaxpr/psum | solution.py:16
Sparse Core Ops, SparseCore 0:
  58.6 87.0 all-reduce.2
  198.0 90.2 all-reduce.2
  346.1 90.2 all-reduce.2
  488.5 90.2 all-reduce.2
  636.3 90.2 all-reduce.2
  778.7 90.2 all-reduce.2
  926.8 90.2 all-reduce.2
  1069.5 90.2 all-reduce.2
  1217.6 90.2 all-reduce.2
  1360.0 90.2 all-reduce.2
  1508.1 90.2 all-reduce.2
  1650.5 90.2 all-reduce.2
  1798.6 90.2 all-reduce.2
  1941.0 90.2 all-reduce.2
  2088.8 90.2 all-reduce.2
  2230.5 90.2 all-reduce.2
where the time goes:
time: 2390 us; the launch traced here: 2380 us
  waiting for transfers between devices  1490 us (62%)
  local copies, waits for them, and re-layouts  572 us (24%)
  matrix products  192 us (8%)
  other arithmetic  77.3 us (3%)
  blocking collectives  36.6 us (2%)
    psum x16, waiting for transfers between devices, spread(): return lax.psum(jnp.where(mine, value, jnp.zeros_like(value)), axis)  1490 us
    dot_general x64, local copies, waits for them, and re-layouts, product(): jnp.einsum('wif,wjf->ijf', left, right, preferred_element_type=jnp.float32)  327 us
    dynamic_update_slice x16, local copies, waits for them, and re-layouts, visit(): lax.dynamic_update_slice(current, block, (jnp.int32(0), jnp.int32(0), sta...  211 us
    dot_general x64, matrix products, product(): jnp.einsum('wif,wjf->ijf', left, right, preferred_element_type=jnp.float32)  174 us
    sub x16, other arithmetic, pair_block(): imag_sum = product(own_imag, other_real) - product(own_real, other_imag)  60.6 us
  transfers between devices with their start and end apart: 16, of which 16 were waited for; matrix products, arithmetic and copies ran while one was open for 0% of the time, Pallas kernels for 0%

commit v1 on v0

--- a/solution.py
+++ b/solution.py
@@ -13,7 +13,10 @@
 
 def spread(value, axis, root):
     mine = lax.axis_index(axis) == root
-    return lax.psum(jnp.where(mine, value, jnp.zeros_like(value)), axis)
+    play_tails_all = lambda vector, mesh_name: jnp.sum(
+        lax.all_gather(vector, axis_name=mesh_name), axis=0
+    )
+    return play_tails_all(jnp.where(mine, value, jnp.zeros_like(value)), axis)
 
 
 def forward_table(width, bins):

time: 2390 us -> 1740 us (0.73)
  waiting for transfers between devices: 1490 us -> 810 us
  other arithmetic: 77.3 us -> 125 us
    psum x16 -> x0, waiting for transfers between devices: 1490 us -> none  [spread(): return lax.psum(jnp.where(mine, value, jnp.zeros_like(value)), axis)]
    all_gather x0 -> x16, waiting for transfers between devices: none -> 809 us  [spread(): lax.all_gather(vector, axis_name=mesh_name)]
    reduce_sum x0 -> x16, other arithmetic: none -> 47.7 us  [spread(): jnp.sum(lax.all_gather(vector, axis_name=mesh_name), axis=0)]
where the time goes in v1:
time: 1740 us; the launch traced here: 1730 us
  waiting for transfers between devices  810 us (47%)
  local copies, waits for them, and re-layouts  556 us (32%)
  matrix products  192 us (11%)
  other arithmetic  125 us (7%)
  blocking collectives  36.6 us (2%)
    all_gather x16, waiting for transfers between devices, spread(): lax.all_gather(vector, axis_name=mesh_name)  809 us
    dot_general x64, local copies, waits for them, and re-layouts, product(): jnp.einsum('wif,wjf->ijf', left, right, preferred_element_type=jnp.float32)  327 us
    dynamic_update_slice x16, local copies, waits for them, and re-layouts, visit(): lax.dynamic_update_slice(current, block, (jnp.int32(0), jnp.int32(0), sta...  211 us
    dot_general x64, matrix products, product(): jnp.einsum('wif,wjf->ijf', left, right, preferred_element_type=jnp.float32)  174 us
    sub x16, other arithmetic, pair_block(): imag_sum = product(own_imag, other_real) - product(own_real, other_imag)  60.6 us
    reduce_sum x16, other arithmetic, spread(): jnp.sum(lax.all_gather(vector, axis_name=mesh_name), axis=0)  47.7 us
    psum x1, blocking collectives, shards(): lax.psum((jnp.sum(traces * good[:, None], axis=0), jnp.sum(good)), 'chan')  36.6 us
  transfers between devices with their start and end apart: 16, of which 16 were waited for; matrix products, arithmetic and copies ran while one was open for 0% of the time, Pallas kernels for 0%

profile of v1, /device:TPU:0, one launch (start us, length us, event | category | flops | bytes accessed | tf_op | source)
XLA Modules:
  0.0 1734.5 jit_solution(2654132772915028153)
XLA Ops:
  9.5 36.6 %all-reduce = (f32[1152]{0:T(1024)S(1)}, f32[]{:T(128)}) all-reduce(f32[1152]{0:T(1024)S(1)} %multiply_reduce_fusion, f32[]{:T(128)} %convert_reduce_fusion), channel_id=1, replica_groups=mesh['groups'=2,'chan'=16] {'chan'}, use_global_device_ids=true, to_apply=%region_1.0 | all-reduce | flops 1153 | bytes 9224 | tf_op jit(solution)/shard_map/psum | solution.py:60
  54.7 1673.2 %while.15 = (s32[]{:T(128)}, bf16[64,64,1024]{2,1,0:T(8,128)(2,1)}, bf16[8,64,256]{1,0,2:T(8,128)(2,1)S(1)}, bf16[256,64]{0,1:T(8,128)(2,1)S(1)}, s32[]{:T(128)}...) while((s32[]{:T(128)}, bf16[64,64,1024]{2,1,0:T(8,128)(2,1)}, ...), condition=%wide.region_7.8_spmd, body=%wide.region_5.7_spmd.sunk | while | flops 174325760 | bytes 65568988 | solution.py:85
  55.8 49.5 %all-gather.5.cloned.1.call-done = bf16[128,64,256]{2,1,0:T(8,128)(2,1)} async-done(((bf16[8,64,256]{2,1,0:T(8,128)(2,1)}), bf16[128,64,256]{2,1,0:T(8,128)(2,1)}) %all-gather.5.cloned.1.call-update) | async-done | bytes 4194320 | tf_op jit(solution)/shard_map/while/body/eval_jaxpr/all_gather | solution.py:17
  124.1 5.4 copy.42
  145.0 10.6 dynamic_update_slice.11
  156.7 50.8 %all-gather.5.cloned.1.call-done = bf16[128,64,256]{2,1,0:T(8,128)(2,1)} async-done(((bf16[8,64,256]{2,1,0:T(8,128)(2,1)}), bf16[128,64,256]{2,1,0:T(8,128)(2,1)}) %all-gather.5.cloned.1.call-update) | async-done | bytes 4194320 | tf_op jit(solution)/shard_map/while/body/eval_jaxpr/all_gather | solution.py:17
  226.3 5.4 copy.42
  247.2 16.0 dynamic_update_slice.11
  264.3 50.8 %all-gather.5.cloned.1.call-done = bf16[128,64,256]{2,1,0:T(8,128)(2,1)} async-done(((bf16[8,64,256]{2,1,0:T(8,128)(2,1)}), bf16[128,64,256]{2,1,0:T(8,128)(2,1)}) %all-gather.5.cloned.1.call-update) | async-done | bytes 4194320 | tf_op jit(solution)/shard_map/while/body/eval_jaxpr/all_gather | solution.py:17
  334.0 5.4 copy.42
  354.8 10.6 dynamic_update_slice.11
  366.5 50.5 %all-gather.5.cloned.1.call-done = bf16[128,64,256]{2,1,0:T(8,128)(2,1)} async-done(((bf16[8,64,256]{2,1,0:T(8,128)(2,1)}), bf16[128,64,256]{2,1,0:T(8,128)(2,1)}) %all-gather.5.cloned.1.call-update) | async-done | bytes 4194320 | tf_op jit(solution)/shard_map/while/body/eval_jaxpr/all_gather | solution.py:17
  435.8 5.4 copy.42
  456.7 16.0 dynamic_update_slice.11
  473.8 50.5 %all-gather.5.cloned.1.call-done = bf16[128,64,256]{2,1,0:T(8,128)(2,1)} async-done(((bf16[8,64,256]{2,1,0:T(8,128)(2,1)}), bf16[128,64,256]{2,1,0:T(8,128)(2,1)}) %all-gather.5.cloned.1.call-update) | async-done | bytes 4194320 | tf_op jit(solution)/shard_map/while/body/eval_jaxpr/all_gather | solution.py:17
  543.1 5.4 copy.42
  564.0 10.6 dynamic_update_slice.11
  575.7 50.5 %all-gather.5.cloned.1.call-done = bf16[128,64,256]{2,1,0:T(8,128)(2,1)} async-done(((bf16[8,64,256]{2,1,0:T(8,128)(2,1)}), bf16[128,64,256]{2,1,0:T(8,128)(2,1)}) %all-gather.5.cloned.1.call-update) | async-done | bytes 4194320 | tf_op jit(solution)/shard_map/while/body/eval_jaxpr/all_gather | solution.py:17
  645.0 5.4 copy.42
  665.9 16.0 dynamic_update_slice.11
  683.0 50.8 %all-gather.5.cloned.1.call-done = bf16[128,64,256]{2,1,0:T(8,128)(2,1)} async-done(((bf16[8,64,256]{2,1,0:T(8,128)(2,1)}), bf16[128,64,256]{2,1,0:T(8,128)(2,1)}) %all-gather.5.cloned.1.call-update) | async-done | bytes 4194320 | tf_op jit(solution)/shard_map/while/body/eval_jaxpr/all_gather | solution.py:17
  752.6 5.4 copy.42
  773.5 10.6 dynamic_update_slice.11
  785.1 50.8 %all-gather.5.cloned.1.call-done = bf16[128,64,256]{2,1,0:T(8,128)(2,1)} async-done(((bf16[8,64,256]{2,1,0:T(8,128)(2,1)}), bf16[128,64,256]{2,1,0:T(8,128)(2,1)}) %all-gather.5.cloned.1.call-update) | async-done | bytes 4194320 | tf_op jit(solution)/shard_map/while/body/eval_jaxpr/all_gather | solution.py:17
  854.8 5.4 copy.42
  875.7 16.0 dynamic_update_slice.11
  892.8 50.8 %all-gather.5.cloned.1.call-done = bf16[128,64,256]{2,1,0:T(8,128)(2,1)} async-done(((bf16[8,64,256]{2,1,0:T(8,128)(2,1)}), bf16[128,64,256]{2,1,0:T(8,128)(2,1)}) %all-gather.5.cloned.1.call-update) | async-done | bytes 4194320 | tf_op jit(solution)/shard_map/while/body/eval_jaxpr/all_gather | solution.py:17
  962.4 5.4 copy.42
  983.3 10.6 dynamic_update_slice.11
  995.0 50.5 %all-gather.5.cloned.1.call-done = bf16[128,64,256]{2,1,0:T(8,128)(2,1)} async-done(((bf16[8,64,256]{2,1,0:T(8,128)(2,1)}), bf16[128,64,256]{2,1,0:T(8,128)(2,1)}) %all-gather.5.cloned.1.call-update) | async-done | bytes 4194320 | tf_op jit(solution)/shard_map/while/body/eval_jaxpr/all_gather | solution.py:17
  1064.3 5.4 copy.42
  1085.2 16.0 dynamic_update_slice.11
  1102.3 50.8 %all-gather.5.cloned.1.call-done = bf16[128,64,256]{2,1,0:T(8,128)(2,1)} async-done(((bf16[8,64,256]{2,1,0:T(8,128)(2,1)}), bf16[128,64,256]{2,1,0:T(8,128)(2,1)}) %all-gather.5.cloned.1.call-update) | async-done | bytes 4194320 | tf_op jit(solution)/shard_map/while/body/eval_jaxpr/all_gather | solution.py:17
  1171.9 5.4 copy.42
  1192.8 10.6 dynamic_update_slice.11
  1204.5 50.5 %all-gather.5.cloned.1.call-done = bf16[128,64,256]{2,1,0:T(8,128)(2,1)} async-done(((bf16[8,64,256]{2,1,0:T(8,128)(2,1)}), bf16[128,64,256]{2,1,0:T(8,128)(2,1)}) %all-gather.5.cloned.1.call-update) | async-done | bytes 4194320 | tf_op jit(solution)/shard_map/while/body/eval_jaxpr/all_gather | solution.py:17
  1273.8 5.4 copy.42
  1294.7 16.0 dynamic_update_slice.11
  1311.8 50.8 %all-gather.5.cloned.1.call-done = bf16[128,64,256]{2,1,0:T(8,128)(2,1)} async-done(((bf16[8,64,256]{2,1,0:T(8,128)(2,1)}), bf16[128,64,256]{2,1,0:T(8,128)(2,1)}) %all-gather.5.cloned.1.call-update) | async-done | bytes 4194320 | tf_op jit(solution)/shard_map/while/body/eval_jaxpr/all_gather | solution.py:17
  1402.3 10.6 dynamic_update_slice.11
  1413.9 50.5 %all-gather.5.cloned.1.call-done = bf16[128,64,256]{2,1,0:T(8,128)(2,1)} async-done(((bf16[8,64,256]{2,1,0:T(8,128)(2,1)}), bf16[128,64,256]{2,1,0:T(8,128)(2,1)}) %all-gather.5.cloned.1.call-update) | async-done | bytes 4194320 | tf_op jit(solution)/shard_map/while/body/eval_jaxpr/all_gather | solution.py:17
  1504.2 16.0 dynamic_update_slice.11
  1521.3 50.5 %all-gather.5.cloned.1.call-done = bf16[128,64,256]{2,1,0:T(8,128)(2,1)} async-done(((bf16[8,64,256]{2,1,0:T(8,128)(2,1)}), bf16[128,64,256]{2,1,0:T(8,128)(2,1)}) %all-gather.5.cloned.1.call-update) | async-done | bytes 4194320 | tf_op jit(solution)/shard_map/while/body/eval_jaxpr/all_gather | solution.py:17
  1590.6 5.4 copy.42
  1611.5 9.9 dynamic_update_slice.11
  1622.4 50.5 %all-gather.5.cloned.1.call-done = bf16[128,64,256]{2,1,0:T(8,128)(2,1)} async-done(((bf16[8,64,256]{2,1,0:T(8,128)(2,1)}), bf16[128,64,256]{2,1,0:T(8,128)(2,1)}) %all-gather.5.cloned.1.call-update) | async-done | bytes 4194320 | tf_op jit(solution)/shard_map/while/body/eval_jaxpr/all_gather | solution.py:17
  1691.8 5.4 copy.42
  1712.6 15.3 dynamic_update_slice.11
  (296 shorter events, 587.0 us)
Async XLA Ops:
  54.7 50.6 %all-gather.5.cloned.1.call-start = ((), (), s32[]{:S(2)}) async-start(), calls=%async_computation | async-start | bytes 4456448 | tf_op jit(solution)/shard_map/while/body/eval_jaxpr/all_gather | solution.py:17
  155.6 51.9 %all-gather.5.cloned.1.call-start = ((), (), s32[]{:S(2)}) async-start(), calls=%async_computation | async-start | bytes 4456448 | tf_op jit(solution)/shard_map/while/body/eval_jaxpr/all_gather | solution.py:17
  263.2 51.9 %all-gather.5.cloned.1.call-start = ((), (), s32[]{:S(2)}) async-start(), calls=%async_computation | async-start | bytes 4456448 | tf_op jit(solution)/shard_map/while/body/eval_jaxpr/all_gather | solution.py:17
  365.4 51.6 %all-gather.5.cloned.1.call-start = ((), (), s32[]{:S(2)}) async-start(), calls=%async_computation | async-start | bytes 4456448 | tf_op jit(solution)/shard_map/while/body/eval_jaxpr/all_gather | solution.py:17
  472.7 51.6 %all-gather.5.cloned.1.call-start = ((), (), s32[]{:S(2)}) async-start(), calls=%async_computation | async-start | bytes 4456448 | tf_op jit(solution)/shard_map/while/body/eval_jaxpr/all_gather | solution.py:17
  574.6 51.6 %all-gather.5.cloned.1.call-start = ((), (), s32[]{:S(2)}) async-start(), calls=%async_computation | async-start | bytes 4456448 | tf_op jit(solution)/shard_map/while/body/eval_jaxpr/all_gather | solution.py:17
  681.9 51.9 %all-gather.5.cloned.1.call-start = ((), (), s32[]{:S(2)}) async-start(), calls=%async_computation | async-start | bytes 4456448 | tf_op jit(solution)/shard_map/while/body/eval_jaxpr/all_gather | solution.py:17
  784.1 51.9 %all-gather.5.cloned.1.call-start = ((), (), s32[]{:S(2)}) async-start(), calls=%async_computation | async-start | bytes 4456448 | tf_op jit(solution)/shard_map/while/body/eval_jaxpr/all_gather | solution.py:17
  891.7 51.9 %all-gather.5.cloned.1.call-start = ((), (), s32[]{:S(2)}) async-start(), calls=%async_computation | async-start | bytes 4456448 | tf_op jit(solution)/shard_map/while/body/eval_jaxpr/all_gather | solution.py:17
  993.9 51.6 %all-gather.5.cloned.1.call-start = ((), (), s32[]{:S(2)}) async-start(), calls=%async_computation | async-start | bytes 4456448 | tf_op jit(solution)/shard_map/while/body/eval_jaxpr/all_gather | solution.py:17
  1101.2 51.9 %all-gather.5.cloned.1.call-start = ((), (), s32[]{:S(2)}) async-start(), calls=%async_computation | async-start | bytes 4456448 | tf_op jit(solution)/shard_map/while/body/eval_jaxpr/all_gather | solution.py:17
  1203.4 51.6 %all-gather.5.cloned.1.call-start = ((), (), s32[]{:S(2)}) async-start(), calls=%async_computation | async-start | bytes 4456448 | tf_op jit(solution)/shard_map/while/body/eval_jaxpr/all_gather | solution.py:17
  1310.7 51.9 %all-gather.5.cloned.1.call-start = ((), (), s32[]{:S(2)}) async-start(), calls=%async_computation | async-start | bytes 4456448 | tf_op jit(solution)/shard_map/while/body/eval_jaxpr/all_gather | solution.py:17
  1412.9 51.6 %all-gather.5.cloned.1.call-start = ((), (), s32[]{:S(2)}) async-start(), calls=%async_computation | async-start | bytes 4456448 | tf_op jit(solution)/shard_map/while/body/eval_jaxpr/all_gather | solution.py:17
  1520.2 51.6 %all-gather.5.cloned.1.call-start = ((), (), s32[]{:S(2)}) async-start(), calls=%async_computation | async-start | bytes 4456448 | tf_op jit(solution)/shard_map/while/body/eval_jaxpr/all_gather | solution.py:17
  1621.3 51.6 %all-gather.5.cloned.1.call-start = ((), (), s32[]{:S(2)}) async-start(), calls=%async_computation | async-start | bytes 4456448 | tf_op jit(solution)/shard_map/while/body/eval_jaxpr/all_gather | solution.py:17
Sparse Core Ops, SparseCore 0:
  57.7 47.6 all-gather.4
  158.5 48.9 all-gather.4
  266.2 48.8 all-gather.4
  368.0 48.8 all-gather.4
  475.4 48.8 all-gather.4
  577.2 48.8 all-gather.4
  684.9 48.8 all-gather.4
  787.0 48.9 all-gather.4
  894.7 48.8 all-gather.4
  996.5 48.8 all-gather.4
  1104.2 48.8 all-gather.4
  1206.0 48.8 all-gather.4
  1313.7 48.8 all-gather.4
  1415.5 48.9 all-gather.4
  1522.8 48.8 all-gather.4
  1624.0 48.8 all-gather.4
